TPU v7x, 256 devices: a whole 4x4x8 slice. The times are simulated.
256 devices in a mesh: rep: 4 (over x), gx: 8 (over z), gy: 8 (over y, core).
Axes of the slice: x: 4, y: 4, z: 8, core: 2. Of those that a mesh axis runs over, the one named last changes fastest.
Arguments:
- features: bfloat16 [4, 8, 8, 512, 128], P('rep', 'gx', 'gy'), may hold values from -6 to 6
- species: int32 [4, 8, 8, 512], P('rep', 'gx', 'gy'), may hold values from 0 to 2
- atom_nbr: int32 [4, 8, 8, 512, 32], P('rep', 'gx', 'gy'), may hold values from 0 to 1535, as said below
- atom_nbr_count: int32 [4, 8, 8, 512], P('rep', 'gx', 'gy'), may hold values from 16 to 32
- atom_dist: float32 [4, 8, 8, 512, 32], P('rep', 'gx', 'gy'), may hold values from 0.8 to 3.9
- send_list: int32 [4, 8, 8, 8, 128], P('rep', 'gx', 'gy'), may hold values from 0 to 511
- probe_nbr: int32 [4, 8, 8, 1024, 32], P('rep', 'gx', 'gy'), may hold values from 0 to 1535, as said below
- probe_dist: float32 [4, 8, 8, 1024, 32], P('rep', 'gx', 'gy'), may hold values from 0.3 to 3.9
- probe_count: int32 [4, 8, 8], P('rep', 'gx', 'gy'), may hold values from 128 to 1024, as said below
- d_density: float32 [4, 8, 8, 1024], P('rep', 'gx', 'gy'), may hold values from -0.03 to 0.03
- species_gain: float32 [3, 128], replicated, may hold values from 0.1 to 1.9
- proj_input: bfloat16 [128, 128], replicated, may hold values from -0.5 to 0.5
- atom_radial: bfloat16 [20, 128], replicated, may hold values from -4 to 4
- atom_filter: bfloat16 [128, 128], replicated, may hold values from -0.5 to 0.5
- mix_first: bfloat16 [128, 128], replicated, may hold values from -0.5 to 0.5
- mix_second: bfloat16 [128, 128], replicated, may hold values from -0.5 to 0.5
- proj_probe: bfloat16 [128, 128], replicated, may hold values from -0.5 to 0.5
- probe_radial: bfloat16 [20, 128], replicated, may hold values from -4 to 4
- probe_filter: bfloat16 [128, 128], replicated, may hold values from -0.5 to 0.5
- read_weight: bfloat16 [128, 128], replicated, may hold values from -0.5 to 0.5
- final_weight: float32 [128], replicated, may hold values from -0.5 to 0.5
Outputs:
- d_features: float32 [4, 8, 8, 512, 128], P('rep', 'gx', 'gy')
- grad_square: float32 [7, 128, 128], replicated
- grad_radial: float32 [2, 20, 128], replicated
- grad_vector: float32 [4, 128], replicated
Inputs may be any that keep to these rules, and one draw needn't show every extreme that they name: `atom_nbr`: entries below 512 name the tile's own atoms; entry 512 + k * 128 + g names row g of ghost block k. About a quarter of the entries name ghost rows. `probe_nbr`: same layout as atom_nbr. About a quarter of the entries name ghost rows. `probe_count`: equal to 1024 on at least one tile of every draw.
All inputs are finite; a program needn't handle non-finite values.
Results may differ from a plain program's by a relative error of at most 0.014.
Values may be sent and summed in bfloat16 or wider, within the bound.
No kernel may reach another device: no remote copies, remote signals or barrier semaphores. Data moves between devices by JAX's collectives and lax.ppermute only.
A program may use at most 64 MiB of HBM per device.

v0:
```python
import math

import jax
import jax.numpy as jnp
from jax import lax
from jax.sharding import PartitionSpec as P

cutoff_radius = 4.0


def with_halo(block, sides, width):
    for axis, dim in sides:
        count = lax.axis_size(axis)
        forward = [(i, i + 1) for i in range(count - 1)]
        forward.append((count - 1, 0))
        backward = [(target, source) for source, target in forward]
        low = lax.ppermute(
            lax.slice_in_dim(block, block.shape[dim] - width, None, axis=dim), axis, forward
        )
        high = lax.ppermute(lax.slice_in_dim(block, 0, width, axis=dim), axis, backward)
        block = jnp.concatenate([low, block, high], axis=dim)
    return block


def shifted_plus(values):
    return jax.nn.softplus(values) - math.log(2.0)


def contract_rows(former, latter):
    return lax.dot_general(
        former, latter, (((0,), (0,)), ((), ())), preferred_element_type=jnp.float32
    )


def contract_cols(former, latter):
    return lax.dot_general(
        former, latter, (((1,), (1,)), ((), ())), preferred_element_type=jnp.float32
    )


def edge_setup(indices, distances, live_mask, row_table, radial_weight, filter_weight):
    flat_dist = distances.reshape(-1)
    spacing = cutoff_radius / (radial_weight.shape[0] - 1)
    centers = jnp.arange(radial_weight.shape[0], dtype=jnp.float32) * spacing
    scaled = (flat_dist[None, :] - centers[:, None]) / spacing
    expansion = jnp.exp(-scaled * scaled).astype(jnp.bfloat16)
    pre_act = contract_rows(expansion, radial_weight)
    hidden = shifted_plus(pre_act).astype(jnp.bfloat16)
    envelope = 0.5 * (jnp.cos(math.pi * flat_dist / cutoff_radius) + 1.0) * live_mask.reshape(-1)
    filters = jnp.dot(hidden, filter_weight, preferred_element_type=jnp.float32) * envelope[:, None]
    gathered = row_table[indices.reshape(-1)].astype(jnp.float32)
    return (expansion, pre_act, hidden, envelope, filters, gathered)


def edge_sums(stored, slot_count):
    filters = stored[4]
    gathered = stored[5]
    terms = (gathered * filters).reshape(-1, slot_count, filters.shape[1])
    return jnp.sum(terms, axis=1)


def edge_backward(stored, indices, filter_weight, grad_message, totals):
    expansion, pre_act, hidden, envelope, filters, gathered = stored
    grad_table, grad_radial, grad_filter = totals
    feature_width = grad_message.shape[1]
    spread = jnp.broadcast_to(
        grad_message[:, None, :], (grad_message.shape[0], indices.shape[1], feature_width)
    ).reshape(-1, feature_width)
    grad_table = grad_table.at[indices.reshape(-1)].add(spread * filters)
    grad_out = (spread * gathered * envelope[:, None]).astype(jnp.bfloat16)
    grad_filter = grad_filter + contract_rows(hidden, grad_out)
    grad_pre = (contract_cols(grad_out, filter_weight) * jax.nn.sigmoid(pre_act)).astype(
        jnp.bfloat16
    )
    grad_radial = grad_radial + jnp.dot(expansion, grad_pre, preferred_element_type=jnp.float32)
    return (grad_table, grad_radial, grad_filter)


def slot_mask(counts, slot_count):
    return (jnp.arange(slot_count, dtype=jnp.int32)[None, :] < counts[:, None]).astype(jnp.float32)


def atom_messages(indices, distances, counts, row_table, radial_weight, filter_weight):
    atom_count, slot_count = indices.shape
    block_rows = min(64, atom_count)
    pieces = (
        indices.reshape(-1, block_rows, slot_count),
        distances.reshape(-1, block_rows, slot_count),
        slot_mask(counts, slot_count).reshape(-1, block_rows, slot_count),
    )

    def one_block(portion):
        stored = edge_setup(
            portion[0], portion[1], portion[2], row_table, radial_weight, filter_weight
        )
        return edge_sums(stored, slot_count)

    return lax.map(one_block, pieces).reshape(atom_count, -1)


def atom_backward(
    indices, distances, counts, row_table, radial_weight, filter_weight, grad_message
):
    atom_count, slot_count = indices.shape
    block_rows = min(64, atom_count)
    pieces = (
        indices.reshape(-1, block_rows, slot_count),
        distances.reshape(-1, block_rows, slot_count),
        slot_mask(counts, slot_count).reshape(-1, block_rows, slot_count),
        grad_message.reshape(-1, block_rows, grad_message.shape[1]),
    )
    initial = (
        jnp.zeros(row_table.shape, jnp.float32),
        jnp.zeros(radial_weight.shape, jnp.float32),
        jnp.zeros(filter_weight.shape, jnp.float32),
    )

    def advance(totals, portion):
        stored = edge_setup(
            portion[0], portion[1], portion[2], row_table, radial_weight, filter_weight
        )
        return (edge_backward(stored, portion[0], filter_weight, portion[3], totals), None)

    return lax.scan(advance, initial, pieces)[0]


def probe_block(
    totals,
    indices,
    distances,
    cotangent,
    row_table,
    probe_radial,
    probe_filter,
    read_weight,
    final_weight,
):
    grad_table, grad_radial, grad_filter, grad_read, grad_final = totals
    stored = edge_setup(
        indices,
        distances,
        jnp.ones(indices.shape, jnp.float32),
        row_table,
        probe_radial,
        probe_filter,
    )
    packed = edge_sums(stored, indices.shape[1]).astype(jnp.bfloat16)
    read_pre = jnp.dot(packed, read_weight, preferred_element_type=jnp.float32)
    grad_final = grad_final + jnp.sum(cotangent[:, None] * shifted_plus(read_pre), axis=0)
    grad_inner = (cotangent[:, None] * final_weight[None, :] * jax.nn.sigmoid(read_pre)).astype(
        jnp.bfloat16
    )
    grad_read = grad_read + contract_rows(packed, grad_inner)
    grad_feats = contract_cols(grad_inner, read_weight)
    edge_totals = edge_backward(
        stored, indices, probe_filter, grad_feats, (grad_table, grad_radial, grad_filter)
    )
    return edge_totals + (grad_read, grad_final)


def interaction_head(atom_feats, kinds, species_gain, proj_input):
    onehot = (kinds[:, None] == jnp.arange(species_gain.shape[0], dtype=jnp.int32)[None, :]).astype(
        jnp.float32
    )
    gains = jnp.dot(onehot, species_gain, precision=lax.Precision.HIGHEST)
    scaled = (atom_feats.astype(jnp.float32) * gains).astype(jnp.bfloat16)
    projected = jnp.dot(scaled, proj_input, preferred_element_type=jnp.float32).astype(jnp.bfloat16)
    return (onehot, gains, scaled, projected)


def interaction_tail(atom_feats, message, mix_first, mix_second, proj_probe):
    packed_msg = message.astype(jnp.bfloat16)
    mix_pre = jnp.dot(packed_msg, mix_first, preferred_element_type=jnp.float32)
    activation = shifted_plus(mix_pre).astype(jnp.bfloat16)
    updated = (
        atom_feats.astype(jnp.float32)
        + jnp.dot(activation, mix_second, preferred_element_type=jnp.float32)
    ).astype(jnp.bfloat16)
    probe_proj = jnp.dot(updated, proj_probe, preferred_element_type=jnp.float32).astype(
        jnp.bfloat16
    )
    return (packed_msg, mix_pre, activation, updated, probe_proj)


def tail_backward(
    grad_proj, packed_msg, mix_pre, activation, updated, mix_first, mix_second, proj_probe
):
    grad_packed = grad_proj.astype(jnp.bfloat16)
    grad_proj_probe = contract_rows(updated, grad_packed)
    grad_updated = contract_cols(grad_packed, proj_probe)
    grad_upd_packed = grad_updated.astype(jnp.bfloat16)
    grad_mix_second = contract_rows(activation, grad_upd_packed)
    grad_mix_pre = (contract_cols(grad_upd_packed, mix_second) * jax.nn.sigmoid(mix_pre)).astype(
        jnp.bfloat16
    )
    grad_mix_first = contract_rows(packed_msg, grad_mix_pre)
    grad_message = contract_cols(grad_mix_pre, mix_first)
    return (grad_updated, grad_message, grad_proj_probe, grad_mix_second, grad_mix_first)


def head_backward(grad_proj, grad_updated, atom_feats, onehot, gains, scaled, proj_input):
    grad_packed = grad_proj.astype(jnp.bfloat16)
    grad_proj_input = contract_rows(scaled, grad_packed)
    grad_scaled = contract_cols(grad_packed, proj_input)
    d_features = grad_updated + grad_scaled * gains
    grad_gain = lax.dot_general(
        onehot,
        grad_scaled * atom_feats.astype(jnp.float32),
        (((0,), (0,)), ((), ())),
        precision=lax.Precision.HIGHEST,
    )
    return (d_features, grad_proj_input, grad_gain)


def add_rows(base, send_rows, returned):
    return base.at[send_rows.reshape(-1)].add(returned.reshape(-1, returned.shape[-1]))


def grid_of(blocks):
    empty = jnp.zeros((1,) + blocks.shape[1:], blocks.dtype)
    return jnp.concatenate([blocks[:4], empty, blocks[4:]], axis=0).reshape(
        (3, 3) + blocks.shape[1:]
    )


def blocks_of(layout):
    flat_grid = layout.reshape((9,) + layout.shape[2:])
    return jnp.concatenate([flat_grid[:4], flat_grid[5:]], axis=0)


def ghost_rows(blocks):
    layout = grid_of(blocks)
    padded = with_halo(layout, (("gx", 0), ("gy", 1)), 1)
    arrived = padded[0::2, 0::2]
    return blocks_of(arrived)


def ghost_grads(blocks):
    layout = grid_of(blocks)
    padded = with_halo(layout.astype(jnp.bfloat16), (("gx", 0), ("gy", 1)), 1).astype(layout.dtype)
    arrived = padded[0::2, 0::2]
    return blocks_of(arrived)


def per_device(
    features,
    species,
    atom_nbr,
    atom_nbr_count,
    atom_dist,
    send_list,
    probe_nbr,
    probe_dist,
    probe_count,
    d_density,
    species_gain,
    proj_input,
    atom_radial,
    atom_filter,
    mix_first,
    mix_second,
    proj_probe,
    probe_radial,
    probe_filter,
    read_weight,
    final_weight,
):
    atom_feats = features[0, 0, 0]
    atom_count = atom_feats.shape[0]
    feature_width = atom_feats.shape[1]
    send_rows = send_list[0, 0, 0]
    tile_nbr = atom_nbr[0, 0, 0]
    tile_dist = atom_dist[0, 0, 0]
    tile_counts = atom_nbr_count[0, 0, 0]
    onehot, gains, scaled, projected = interaction_head(
        atom_feats, species[0, 0, 0], species_gain, proj_input
    )
    row_table = jnp.concatenate(
        [projected, ghost_rows(projected[send_rows]).reshape(-1, feature_width)], axis=0
    )
    message = atom_messages(tile_nbr, tile_dist, tile_counts, row_table, atom_radial, atom_filter)
    packed_msg, mix_pre, activation, updated, probe_proj = interaction_tail(
        atom_feats, message, mix_first, mix_second, proj_probe
    )
    probe_table = jnp.concatenate(
        [probe_proj, ghost_rows(probe_proj[send_rows]).reshape(-1, feature_width)], axis=0
    )
    probe_ids = probe_nbr[0, 0, 0]
    probe_far = probe_dist[0, 0, 0]
    cotangents = d_density[0, 0, 0]
    block_rows = min(64, probe_ids.shape[0])
    active = probe_count[0, 0, 0]
    turns = (active + block_rows - 1) // block_rows
    initial = (
        jnp.zeros(probe_table.shape, jnp.float32),
        jnp.zeros(probe_radial.shape, jnp.float32),
        jnp.zeros(probe_filter.shape, jnp.float32),
        jnp.zeros(read_weight.shape, jnp.float32),
        jnp.zeros(final_weight.shape, jnp.float32),
    )

    def probe_turn(turn_index, totals):
        first_row = turn_index * block_rows
        indices = lax.dynamic_slice_in_dim(probe_ids, first_row, block_rows, 0)
        distances = lax.dynamic_slice_in_dim(probe_far, first_row, block_rows, 0)
        positions = first_row + jnp.arange(block_rows, dtype=jnp.int32)
        cotangent = lax.dynamic_slice_in_dim(cotangents, first_row, block_rows, 0) * (
            positions < active
        ).astype(jnp.float32)
        return probe_block(
            totals,
            indices,
            distances,
            cotangent,
            probe_table,
            probe_radial,
            probe_filter,
            read_weight,
            final_weight,
        )

    grad_ptable, grad_pradial, grad_pfilter, grad_read, grad_final = lax.fori_loop(
        0, turns, probe_turn, initial
    )
    returned_probe = ghost_grads(
        grad_ptable[atom_count:].reshape(send_rows.shape + (feature_width,))
    )
    grad_q = add_rows(grad_ptable[:atom_count], send_rows, returned_probe)
    grad_updated, grad_message, grad_proj_probe, grad_mix_second, grad_mix_first = tail_backward(
        grad_q, packed_msg, mix_pre, activation, updated, mix_first, mix_second, proj_probe
    )
    grad_atable, grad_aradial, grad_afilter = atom_backward(
        tile_nbr, tile_dist, tile_counts, row_table, atom_radial, atom_filter, grad_message
    )
    returned_atom = ghost_grads(
        grad_atable[atom_count:].reshape(send_rows.shape + (feature_width,))
    )
    grad_u = add_rows(grad_atable[:atom_count], send_rows, returned_atom)
    d_features, grad_proj_input, grad_gain = head_backward(
        grad_u, grad_updated, atom_feats, onehot, gains, scaled, proj_input
    )
    (
        grad_pradial,
        grad_pfilter,
        grad_read,
        grad_final,
        grad_aradial,
        grad_afilter,
        grad_proj_input,
        grad_mix_first,
        grad_mix_second,
        grad_proj_probe,
        grad_gain,
    ) = lax.psum(
        (
            grad_pradial,
            grad_pfilter,
            grad_read,
            grad_final,
            grad_aradial,
            grad_afilter,
            grad_proj_input,
            grad_mix_first,
            grad_mix_second,
            grad_proj_probe,
            grad_gain,
        ),
        ("rep", "gx", "gy"),
    )
    grad_square = jnp.stack(
        [
            grad_pfilter,
            grad_read,
            grad_afilter,
            grad_proj_input,
            grad_mix_first,
            grad_mix_second,
            grad_proj_probe,
        ],
        axis=0,
    )
    grad_radial = jnp.stack([grad_pradial, grad_aradial], axis=0)
    grad_vector = jnp.concatenate([grad_final[None, :], grad_gain], axis=0)
    return (d_features[None, None, None], grad_square, grad_radial, grad_vector)


def solution(mesh):
    in_specs = (
        P("rep", "gx", "gy", None, None),
        P("rep", "gx", "gy", None),
        P("rep", "gx", "gy", None, None),
        P("rep", "gx", "gy", None),
        P("rep", "gx", "gy", None, None),
        P("rep", "gx", "gy", None, None),
        P("rep", "gx", "gy", None, None),
        P("rep", "gx", "gy", None, None),
        P("rep", "gx", "gy"),
        P("rep", "gx", "gy", None),
        P(),
        P(),
        P(),
        P(),
        P(),
        P(),
        P(),
        P(),
        P(),
        P(),
        P(),
    )
    out_specs = (P("rep", "gx", "gy", None, None), P(), P(), P())
    return jax.shard_map(
        per_device, mesh=mesh, in_specs=in_specs, out_specs=out_specs, check_vma=False
    )
```

profile of v0, /device:TPU:20, one launch (start us, length us, event | category | flops | bytes accessed | tf_op | source)
XLA Modules:
  0.0 1230.2 jit_solution(3619907784118653418)
XLA Ops:
  26.9 67.8 %while.50 = (s32[]{:T(128)}, bf16[8,64,128]{2,1,0:T(8,128)(2,1)S(1)}, s32[8,64,32]{2,1,0:T(8,128)S(1)}, bf16[1536,128]{1,0:T(8,128)(2,1)S(1)}, f32[8,64,32]{2,1,...) while((s32[]{:T(128)}, ...), condition=%wide.region_2.3_spmd, body=%wide.region_0.2_spmd.sunk | while | flops 80953368 | bytes 1840393 | solution.py:98
  28.1 6.2 gather_fusion
  61.9 6.2 gather_fusion
  87.4 6.2 gather_fusion
  114.4 231.5 %while.51 = (s32[]{:T(128)}, f32[1536,128]{1,0:T(8,128)S(1)}, f32[20,128]{1,0:T(8,128)}, f32[128,128]{1,0:T(8,128)}, f32[128,128]{1,0:T(8,128)}, /*index=5*/f32[...) while((s32[]{:T(128)}, f32[1536,128]{1,0:T(8,128)S(1)}, ...), condition=%wide.region_7.8_spmd, body=%wide.region_3.7_spmd.sunk | while | flops 237339360 | bytes 26602296 | solution.py:322
  133.7 11.8 scatter_fusion
  150.2 6.2 gather_fusion.1
  166.8 11.8 scatter_fusion
  183.3 6.2 gather_fusion.1
  199.9 11.8 scatter_fusion
  233.0 11.8 scatter_fusion
  266.1 11.8 scatter_fusion
  299.1 11.8 scatter_fusion
  315.6 6.2 gather_fusion.1
  332.2 11.8 scatter_fusion
  346.1 36.6 %collective-permute-start.9 = (bf16[1,3,128,128]{3,2,1,0:T(8,128)(2,1)S(1)}, bf16[1,3,128,128]{3,2,1,0:T(8,128)(2,1)S(1)}, u32[]{:S(2)}, u32[]{:S(2)}) collective-permute-start(bf16[1,3,128,128]{3,2,1,0:T(8,128)(2,1)S(1)} %bitcast.224), channel_id=1, source_target_pairs={{8,0},{16,8},{24,16},{32,24},{40,32},{48,40},{56,48},{0,56},{9,1},... | collective-permute-start | bytes 294920 | tf_op jit(solution)/shard_map/ppermute | solution.py:20
  387.1 264.8 %collective-permute-start.11 = (bf16[5,1,128,128]{3,2,1,0:T(8,128)(2,1)S(1)}, bf16[5,1,128,128]{3,2,1,0:T(8,128)(2,1)S(1)}, u32[]{:S(2)}, u32[]{:S(2)}) collective-permute-start(bf16[5,1,128,128]{3,2,1,0:T(8,128)(2,1)S(1)} %get-tuple-element.639), channel_id=1, source_target_pairs={{1,0},{2,1},{3,2},{4,3},{5,4},{6,5},{7,6},{0,7},{9,8},{10,9},{11,1... | collective-permute-start | bytes 491528 | tf_op jit(solution)/shard_map/ppermute | solution.py:20
  655.2 6.4 scatter_fusion.2
  665.0 197.2 %while.52 = (s32[]{:T(128)}, f32[1536,128]{1,0:T(8,128)S(1)}, f32[20,128]{1,0:T(8,128)S(1)}, f32[128,128]{1,0:T(8,128)}, s32[8,64,32]{2,1,0:T(8,128)}, /*index=5...) while((s32[]{:T(128)}, f32[1536,128]{1,0:T(8,128)S(1)}, ...), condition=%wide.region_11.12_spmd.clone, body=%wide.region_9.11_spmd.clone.sunk | while | flops 230102048 | bytes 15238644 | solution.py:124
  669.0 11.8 scatter_fusion.1
  680.8 6.2 gather_fusion.2
  693.6 11.8 scatter_fusion.1
  718.2 11.8 scatter_fusion.1
  742.9 11.8 scatter_fusion.1
  767.5 11.8 scatter_fusion.1
  779.3 6.2 gather_fusion.2
  792.2 11.8 scatter_fusion.1
  816.8 11.8 scatter_fusion.1
  841.5 11.8 scatter_fusion.1
  853.3 6.2 gather_fusion.2
  882.8 79.9 %all-reduce = (f32[1,20,128]{2,1,0:T(8,128)S(1)}, f32[1,20,128]{2,1,0:T(8,128)S(1)}, f32[3,128]{1,0:T(4,128)S(1)}, f32[1,128]{1,0:T(1,128)S(1)}) all-reduce(f32[1,20,128]{2,1,0:T(8,128)S(1)} %bitcast.232, f32[1,20,128]{2,1,0:T(8,128)S(1)} %bitcast.228, ...), channel_id=1, replica_groups=mesh['rep'=4,'gx'=8,'gy'=8] {'rep','gx','gy'}, use_global_device_ids=true, to_apply=%region_21.22 | all-reduce | flops 5632 | bytes 45056 | tf_op jit(solution)/shard_map/psum | solution.py:354
  964.7 252.8 %all-reduce.4.cloned.1.call-done = (f32[1,128,128]{2,1,0:T(8,128)}, f32[1,128,128]{2,1,0:T(8,128)}, f32[1,128,128]{2,1,0:T(8,128)}, f32[1,128,128]{2,1,0:T(8,128...) async-done(((f32[1,128,128]{2,1,0:T(8,128)}, f32[1,128,128]{2,1,0:T(8,128)}, f32[1,128,128]{2,1,0:T(8,128)}, f32[1,128,128]{2,1,0:T(8,128)}, ...) | async-done | bytes 458768 | tf_op jit(solution)/shard_map/psum | solution.py:354
  (866 shorter events, 339.0 us)
Async XLA Ops:
  7.2 89.7 %copy-start = (bf16[128,128]{1,0:T(8,128)(2,1)S(1)}, bf16[128,128]{1,0:T(8,128)(2,1)}, u32[]{:S(2)}) copy-start(bf16[128,128]{1,0:T(8,128)(2,1)} %param.43) | copy-start | bytes 98308
  7.2 1210.3 %all-reduce.4.cloned.1.call-start = ((), (), s32[]{:S(2)}) async-start(), calls=%async_computation | async-start | bytes 917504 | tf_op jit(solution)/shard_map/psum | solution.py:354
  12.4 8.7 collective-permute-start
  14.4 6.7 collective-permute-start.1
  18.5 85.1 %copy-start.59 = (bf16[9]{0:T(256)(128)(2,1)}, bf16[9]{0:T(256)(128)(2,1)S(1)}, u32[]{:S(2)}) copy-start(bf16[9]{0:T(256)(128)(2,1)S(1)} %pad.58.clone) | copy-start | bytes 58
  21.2 4.8 collective-permute-start.2
  21.2 4.7 collective-permute-start.3
  26.9 67.8 %copy-start.37 = (bf16[128,128]{1,0:T(8,128)(2,1)S(1)}, bf16[128,128]{1,0:T(8,128)(2,1)}, u32[]{:S(2)}) copy-start(bf16[128,128]{1,0:T(8,128)(2,1)} %param.41) | copy-start | bytes 98308
  100.4 6.4 collective-permute-start.4
  100.5 6.3 collective-permute-start.5
  106.8 4.8 collective-permute-start.6
  107.2 4.4 collective-permute-start.7
  116.2 7.2 copy-start.3
  133.7 11.8 copy-start.50
  149.3 7.2 copy-start.3
  166.8 11.8 copy-start.50
  182.3 7.2 copy-start.3
  199.9 11.8 copy-start.50
  233.0 11.8 copy-start.50
  266.0 11.8 copy-start.50
  299.1 11.8 copy-start.50
  314.7 7.2 copy-start.3
  332.2 11.8 copy-start.50
  346.1 39.2 %collective-permute-start.8 = (bf16[1,3,128,128]{3,2,1,0:T(8,128)(2,1)S(1)}, bf16[1,3,128,128]{3,2,1,0:T(8,128)(2,1)S(1)}, u32[]{:S(2)}, u32[]{:S(2)}) collective-permute-start(bf16[1,3,128,128]{3,2,1,0:T(8,128)(2,1)S(1)} %bitcast.226), channel_id=1, source_target_pairs={{0,8},{8,16},{16,24},{24,32},{32,40},{40,48},{48,56},{56,0},{1,9},... | collective-permute-start | bytes 294920 | tf_op jit(solution)/shard_map/ppermute | solution.py:17
  346.1 40.9 %collective-permute-start.9 = (bf16[1,3,128,128]{3,2,1,0:T(8,128)(2,1)S(1)}, bf16[1,3,128,128]{3,2,1,0:T(8,128)(2,1)S(1)}, u32[]{:S(2)}, u32[]{:S(2)}) collective-permute-start(bf16[1,3,128,128]{3,2,1,0:T(8,128)(2,1)S(1)} %bitcast.224), channel_id=1, source_target_pairs={{8,0},{16,8},{24,16},{32,24},{40,32},{48,40},{56,48},{0,56},{9,1},... | collective-permute-start | bytes 294920 | tf_op jit(solution)/shard_map/ppermute | solution.py:20
  387.1 264.8 %copy-start.52 = (s32[1,1,1,8,128]{4,3,2,1,0:T(8,128)S(1)}, s32[1,1,1,8,128]{4,3,2,1,0:T(8,128)}, u32[]{:S(2)}) copy-start(s32[1,1,1,8,128]{4,3,2,1,0:T(8,128)} %param.32) | copy-start | bytes 12292
  387.1 267.8 %collective-permute-start.10 = (bf16[5,1,128,128]{3,2,1,0:T(8,128)(2,1)S(1)}, bf16[5,1,128,128]{3,2,1,0:T(8,128)(2,1)S(1)}, u32[]{:S(2)}, u32[]{:S(2)}) collective-permute-start(bf16[5,1,128,128]{3,2,1,0:T(8,128)(2,1)S(1)} %get-tuple-element.638), channel_id=1, source_target_pairs={{0,1},{1,2},{2,3},{3,4},{4,5},{5,6},{6,7},{7,0},{8,9},{9,10},{10,1... | collective-permute-start | bytes 491528 | tf_op jit(solution)/shard_map/ppermute | solution.py:17
  387.1 267.7 %collective-permute-start.11 = (bf16[5,1,128,128]{3,2,1,0:T(8,128)(2,1)S(1)}, bf16[5,1,128,128]{3,2,1,0:T(8,128)(2,1)S(1)}, u32[]{:S(2)}, u32[]{:S(2)}) collective-permute-start(bf16[5,1,128,128]{3,2,1,0:T(8,128)(2,1)S(1)} %get-tuple-element.639), channel_id=1, source_target_pairs={{1,0},{2,1},{3,2},{4,3},{5,4},{6,5},{7,6},{0,7},{9,8},{10,9},{11,1... | collective-permute-start | bytes 491528 | tf_op jit(solution)/shard_map/ppermute | solution.py:20
  862.2 5.9 collective-permute-start.12
  863.0 5.5 collective-permute-start.13
  868.5 4.8 collective-permute-start.14
  869.8 3.5 collective-permute-start.15
  (180 other events, 206.3 us)
Sparse Core Ops, SparseCore 0:
  964.1 253.3 all-reduce.3
where the time goes:
time: 1240 us; the launch traced here: 1230 us
  starting transfers between devices  319 us (26%)
  waiting for transfers between devices  266 us (21%)
  local copies, waits for them, and re-layouts  247 us (20%)
  other arithmetic  211 us (17%)
  matrix products  88.4 us (7%)
  blocking collectives  79.9 us (6%)
  between operations  15.4 us (1%)
    ppermute x8, starting transfers between devices, with_halo(): lax.ppermute(lax.slice_in_dim(block, 0, width, axis=dim), axis, backward)  315 us
    psum x1, waiting for transfers between devices, per_device(): lax.psum((grad_pradial, grad_pfilter, grad_read, grad_final, grad_aradial...  253 us
    scatter-add x15, other arithmetic, edge_backward(): grad_table = grad_table.at[indices.reshape(-1)].add(spread * filters)  177 us
    gather x23, local copies, waits for them, and re-layouts, edge_setup(): gathered = row_table[indices.reshape(-1)].astype(jnp.float32)  142 us
    psum x1, blocking collectives, per_device(): lax.psum((grad_pradial, grad_pfilter, grad_read, grad_final, grad_aradial...  79.9 us
    while x288, local copies, waits for them, and re-layouts  34.6 us
    dot_general x23, matrix products, edge_setup(): jnp.dot(hidden, filter_weight, preferred_element_type=jnp.float32)  27 us
  transfers between devices with their start and end apart: 17, of which 11 were waited for; matrix products, arithmetic and copies ran while one was open for 1% of the time, Pallas kernels for 0%

commit v1 on v0

--- a/solution.py
+++ b/solution.py
@@ -38,6 +38,18 @@
     )
 
 
+def one_hot_rows(indices, row_count):
+    flat = indices.reshape(-1)
+    return (flat[:, None] == jnp.arange(row_count, dtype=jnp.int32)[None, :]).astype(jnp.bfloat16)
+
+
+def scatter_rows(selector, values):
+    high = values.astype(jnp.bfloat16)
+    low = (values - high.astype(jnp.float32)).astype(jnp.bfloat16)
+    both = contract_rows(selector, jnp.concatenate([high, low], axis=1))
+    return both[:, : values.shape[1]] + both[:, values.shape[1] :]
+
+
 def edge_setup(indices, distances, live_mask, row_table, radial_weight, filter_weight):
     flat_dist = distances.reshape(-1)
     spacing = cutoff_radius / (radial_weight.shape[0] - 1)
@@ -48,8 +60,9 @@
     hidden = shifted_plus(pre_act).astype(jnp.bfloat16)
     envelope = 0.5 * (jnp.cos(math.pi * flat_dist / cutoff_radius) + 1.0) * live_mask.reshape(-1)
     filters = jnp.dot(hidden, filter_weight, preferred_element_type=jnp.float32) * envelope[:, None]
-    gathered = row_table[indices.reshape(-1)].astype(jnp.float32)
-    return (expansion, pre_act, hidden, envelope, filters, gathered)
+    selector = one_hot_rows(indices, row_table.shape[0])
+    gathered = jnp.dot(selector, row_table, preferred_element_type=jnp.float32)
+    return (expansion, pre_act, hidden, envelope, filters, gathered, selector)
 
 
 def edge_sums(stored, slot_count):
@@ -60,13 +73,13 @@
 
 
 def edge_backward(stored, indices, filter_weight, grad_message, totals):
-    expansion, pre_act, hidden, envelope, filters, gathered = stored
+    expansion, pre_act, hidden, envelope, filters, gathered, selector = stored
     grad_table, grad_radial, grad_filter = totals
     feature_width = grad_message.shape[1]
     spread = jnp.broadcast_to(
         grad_message[:, None, :], (grad_message.shape[0], indices.shape[1], feature_width)
     ).reshape(-1, feature_width)
-    grad_table = grad_table.at[indices.reshape(-1)].add(spread * filters)
+    grad_table = grad_table + scatter_rows(selector, spread * filters)
     grad_out = (spread * gathered * envelope[:, None]).astype(jnp.bfloat16)
     grad_filter = grad_filter + contract_rows(hidden, grad_out)
     grad_pre = (contract_cols(grad_out, filter_weight) * jax.nn.sigmoid(pre_act)).astype(
@@ -82,7 +95,7 @@
 
 def atom_messages(indices, distances, counts, row_table, radial_weight, filter_weight):
     atom_count, slot_count = indices.shape
-    block_rows = min(64, atom_count)
+    block_rows = min(128, atom_count)
     pieces = (
         indices.reshape(-1, block_rows, slot_count),
         distances.reshape(-1, block_rows, slot_count),
@@ -102,7 +115,7 @@
     indices, distances, counts, row_table, radial_weight, filter_weight, grad_message
 ):
     atom_count, slot_count = indices.shape
-    block_rows = min(64, atom_count)
+    block_rows = min(128, atom_count)
     pieces = (
         indices.reshape(-1, block_rows, slot_count),
         distances.reshape(-1, block_rows, slot_count),
@@ -288,9 +301,15 @@
     probe_ids = probe_nbr[0, 0, 0]
     probe_far = probe_dist[0, 0, 0]
     cotangents = d_density[0, 0, 0]
-    block_rows = min(64, probe_ids.shape[0])
+    block_rows = min(128, probe_ids.shape[0])
     active = probe_count[0, 0, 0]
-    turns = (active + block_rows - 1) // block_rows
+    positions = jnp.arange(probe_ids.shape[0], dtype=jnp.int32)
+    masked = cotangents * (positions < active).astype(jnp.float32)
+    pieces = (
+        probe_ids.reshape(-1, block_rows, probe_ids.shape[1]),
+        probe_far.reshape(-1, block_rows, probe_far.shape[1]),
+        masked.reshape(-1, block_rows),
+    )
     initial = (
         jnp.zeros(probe_table.shape, jnp.float32),
         jnp.zeros(probe_radial.shape, jnp.float32),
@@ -299,28 +318,35 @@
         jnp.zeros(final_weight.shape, jnp.float32),
     )
 
-    def probe_turn(turn_index, totals):
-        first_row = turn_index * block_rows
-        indices = lax.dynamic_slice_in_dim(probe_ids, first_row, block_rows, 0)
-        distances = lax.dynamic_slice_in_dim(probe_far, first_row, block_rows, 0)
-        positions = first_row + jnp.arange(block_rows, dtype=jnp.int32)
-        cotangent = lax.dynamic_slice_in_dim(cotangents, first_row, block_rows, 0) * (
-            positions < active
-        ).astype(jnp.float32)
-        return probe_block(
-            totals,
-            indices,
-            distances,
-            cotangent,
-            probe_table,
-            probe_radial,
-            probe_filter,
-            read_weight,
-            final_weight,
+    def probe_turn(totals, portion):
+        return (
+            probe_block(
+                totals,
+                portion[0],
+                portion[1],
+                portion[2],
+                probe_table,
+                probe_radial,
+                probe_filter,
+                read_weight,
+                final_weight,
+            ),
+            None,
         )
 
-    grad_ptable, grad_pradial, grad_pfilter, grad_read, grad_final = lax.fori_loop(
-        0, turns, probe_turn, initial
+    grad_ptable, grad_pradial, grad_pfilter, grad_read, grad_final = lax.scan(
+        probe_turn, initial, pieces
+    )[0]
+    probe_sums = lax.psum(
+        jnp.concatenate(
+            [
+                grad_pfilter.reshape(-1),
+                grad_read.reshape(-1),
+                grad_pradial.reshape(-1),
+                grad_final.reshape(-1),
+            ]
+        ),
+        ("rep", "gx", "gy"),
     )
     returned_probe = ghost_grads(
         grad_ptable[atom_count:].reshape(send_rows.shape + (feature_width,))
@@ -329,8 +355,15 @@
     grad_updated, grad_message, grad_proj_probe, grad_mix_second, grad_mix_first = tail_backward(
         grad_q, packed_msg, mix_pre, activation, updated, mix_first, mix_second, proj_probe
     )
+    tail_part = jnp.concatenate(
+        [grad_mix_first.reshape(-1), grad_mix_second.reshape(-1), grad_proj_probe.reshape(-1)]
+    )
+    tail_sums = lax.psum(tail_part, ("rep", "gx", "gy"))
     grad_atable, grad_aradial, grad_afilter = atom_backward(
         tile_nbr, tile_dist, tile_counts, row_table, atom_radial, atom_filter, grad_message
+    )
+    grad_atable, probe_sums, tail_sums = lax.optimization_barrier(
+        (grad_atable, probe_sums, tail_sums)
     )
     returned_atom = ghost_grads(
         grad_atable[atom_count:].reshape(send_rows.shape + (feature_width,))
@@ -339,48 +372,31 @@
     d_features, grad_proj_input, grad_gain = head_backward(
         grad_u, grad_updated, atom_feats, onehot, gains, scaled, proj_input
     )
-    (
-        grad_pradial,
-        grad_pfilter,
-        grad_read,
-        grad_final,
-        grad_aradial,
-        grad_afilter,
-        grad_proj_input,
-        grad_mix_first,
-        grad_mix_second,
-        grad_proj_probe,
-        grad_gain,
-    ) = lax.psum(
-        (
-            grad_pradial,
-            grad_pfilter,
-            grad_read,
-            grad_final,
-            grad_aradial,
-            grad_afilter,
-            grad_proj_input,
-            grad_mix_first,
-            grad_mix_second,
-            grad_proj_probe,
-            grad_gain,
-        ),
-        ("rep", "gx", "gy"),
-    )
-    grad_square = jnp.stack(
+    atom_part = jnp.concatenate(
         [
-            grad_pfilter,
-            grad_read,
-            grad_afilter,
-            grad_proj_input,
-            grad_mix_first,
-            grad_mix_second,
-            grad_proj_probe,
-        ],
-        axis=0,
-    )
-    grad_radial = jnp.stack([grad_pradial, grad_aradial], axis=0)
-    grad_vector = jnp.concatenate([grad_final[None, :], grad_gain], axis=0)
+            grad_afilter.reshape(-1),
+            grad_proj_input.reshape(-1),
+            grad_aradial.reshape(-1),
+            grad_gain.reshape(-1),
+        ]
+    )
+    atom_sums = lax.psum(atom_part, ("rep", "gx", "gy"))
+    square = feature_width * feature_width
+    radial = probe_radial.shape[0] * feature_width
+    grad_square = jnp.concatenate(
+        [
+            probe_sums[: 2 * square],
+            atom_sums[:square],
+            atom_sums[square : 2 * square],
+            tail_sums,
+        ]
+    ).reshape(7, feature_width, feature_width)
+    grad_radial = jnp.concatenate(
+        [probe_sums[2 * square : 2 * square + radial], atom_sums[2 * square : 2 * square + radial]]
+    ).reshape(2, -1, feature_width)
+    grad_vector = jnp.concatenate(
+        [probe_sums[2 * square + radial :], atom_sums[2 * square + radial :]]
+    ).reshape(-1, feature_width)
     return (d_features[None, None, None], grad_square, grad_radial, grad_vector)
 
 

time: 1240 us -> 928 us (0.75)
  starting transfers between devices: 319 us -> 23.6 us
  matrix products: 88.4 us -> 350 us
  local copies, waits for them, and re-layouts: 247 us -> 77.2 us
  other arithmetic: 211 us -> 53 us
  waiting for transfers between devices: 266 us -> 385 us
  blocking collectives: 79.9 us -> 0 us
    ppermute x8, starting transfers between devices: 315 us -> 18.1 us  [with_halo(): lax.ppermute(lax.slice_in_dim(block, 0, width, axis=dim), axis, backward)]
    scatter-add x15 -> x0, other arithmetic: 177 us -> none  [edge_backward(): grad_table = grad_table.at[indices.reshape(-1)].add(spread * filters)]
    gather x23 -> x0, local copies, waits for them, and re-layouts: 142 us -> none  [edge_setup(): gathered = row_table[indices.reshape(-1)].astype(jnp.float32)]
    dot_general x41 -> x48, matrix products: 23.2 us -> 150 us  [contract_rows(): lax.dot_general(former, latter, (((0,), (0,)), ((), ())), preferred_eleme...]
    psum x1 -> x2, waiting for transfers between devices: 253 us -> 366 us  [the longest x1 241 us: per_device(): atom_sums = lax.psum(atom_part, ('rep', 'gx', 'gy'))]
    dot_general x0 -> x16, matrix products: none -> 99 us  [edge_setup(): gathered = jnp.dot(selector, row_table, preferred_element_type=jnp.float32)]
    psum x1 -> x0, blocking collectives: 79.9 us -> none  [per_device(): lax.psum((grad_pradial, grad_pfilter, grad_read, grad_final, grad_aradial...]
    dot_general x23 -> x16, matrix products: 27 us -> 51.7 us  [edge_setup(): jnp.dot(hidden, filter_weight, preferred_element_type=jnp.float32)]
  transfers between devices with their start and end apart: 17 -> 18, of which waited for: 11 -> 10; matrix products, arithmetic and copies ran while one was open for 1% -> 14% of each run, Pallas kernels for 0% -> 0%
where the time goes in v1:
time: 928 us; the launch traced here: 919 us
  waiting for transfers between devices  385 us (41%)
  matrix products  350 us (38%)
  local copies, waits for them, and re-layouts  77.2 us (8%)
  other arithmetic  53 us (6%)
  starting transfers between devices  23.6 us (3%)
  between operations  16 us (2%)
  loops' own time  14 us (2%)
    psum x1, waiting for transfers between devices, per_device(): atom_sums = lax.psum(atom_part, ('rep', 'gx', 'gy'))  241 us
    dot_general x48, matrix products, contract_rows(): lax.dot_general(former, latter, (((0,), (0,)), ((), ())), preferred_eleme...  150 us
    psum x1, waiting for transfers between devices, per_device(): lax.psum(jnp.concatenate([grad_pfilter.reshape(-1), grad_read.reshape(-1)...  125 us
    dot_general x16, matrix products, edge_setup(): gathered = jnp.dot(selector, row_table, preferred_element_type=jnp.float32)  99 us
    dot_general x16, matrix products, edge_setup(): jnp.dot(hidden, filter_weight, preferred_element_type=jnp.float32)  51.7 us
    dot_general x12, matrix products, edge_backward(): jnp.dot(expansion, grad_pre, preferred_element_type=jnp.float32)  26 us
    convert_element_type x8, other arithmetic, scatter_rows(): high = values.astype(jnp.bfloat16)  22.2 us
    while x264, local copies, waits for them, and re-layouts  21.3 us
  transfers between devices with their start and end apart: 18, of which 10 were waited for; matrix products, arithmetic and copies ran while one was open for 14% of the time, Pallas kernels for 0%

profile of v1, /device:TPU:20, one launch (start us, length us, event | category | flops | bytes accessed | tf_op | source)
XLA Modules:
  0.0 918.6 jit_solution(9248540030862802442)
XLA Ops:
  28.8 40.1 %while.51 = (s32[]{:T(128)}, bf16[4,128,128]{2,1,0:T(8,128)(2,1)S(1)}, s32[4,128,32]{2,1,0:T(8,128)S(1)}, bf16[1536,128]{1,0:T(8,128)(2,1)S(1)}, f32[4,128,32]{2...) while((s32[]{:T(128)}, ...), condition=%wide.region_2.3_spmd, body=%wide.region_0.2_spmd.sunk | while | flops 1778270208 | bytes 5018889 | solution.py:111
  40.0 5.4 fusion.213
  86.0 289.0 %while.52 = (s32[]{:T(128)}, f32[1536,128]{1,0:T(8,128)}, f32[20,128]{1,0:T(8,128)}, f32[128,128]{1,0:T(8,128)}, f32[128,128]{1,0:T(8,128)}, /*index=5*/f32[128]...) while((s32[]{:T(128)}, f32[1536,128]{1,0:T(8,128)}, ...), condition=%wide.region_6.7_spmd.clone, body=%wide.region_3.6_spmd.clone.sunk | while | flops 5324391424 | bytes 60448700 | solution.py:337
  91.6 6.4 fusion.231
  105.9 7.5 fusion.235
  126.2 6.4 fusion.231
  140.6 7.5 fusion.235
  160.9 6.4 fusion.231
  175.2 7.5 fusion.235
  195.5 6.4 fusion.231
  209.8 7.5 fusion.235
  230.1 6.4 fusion.231
  244.5 7.5 fusion.235
  264.8 6.4 fusion.231
  279.1 7.5 fusion.235
  299.4 6.4 fusion.231
  313.7 7.5 fusion.235
  334.0 6.4 fusion.231
  348.4 7.5 fusion.235
  388.8 6.1 scatter_fusion
  398.1 122.5 %while.53 = (s32[]{:T(128)}, f32[1536,128]{1,0:T(8,128)S(1)}, f32[20,128]{1,0:T(8,128)S(1)}, f32[128,128]{1,0:T(8,128)}, s32[4,128,32]{2,1,0:T(8,128)S(1)}, /*in...) while((s32[]{:T(128)}, f32[1536,128]{1,0:T(8,128)S(1)}, ...), condition=%wide.region_9.10_spmd.clone, body=%wide.region_8.9_spmd.clone.sunk | while | flops 5316695040 | bytes 50439636 | solution.py:137
  409.2 5.9 fusion.251
  416.7 6.5 fusion.253
  439.9 5.9 fusion.251
  447.4 6.5 fusion.253
  470.5 5.9 fusion.251
  478.0 6.5 fusion.253
  501.1 5.9 fusion.251
  508.6 6.5 fusion.253
  520.6 124.7 %all-reduce.6.cloned.1.call-done = (f32[35456]{0:T(1024)}, f32[49152]{0:T(1024)}) async-done(((f32[35456]{0:T(1024)}, f32[49152]{0:T(1024)}), (f32[35456]{0:T(1024)}, f32[49152]{0:T(1024)})) %all-reduce.6.cloned.1.call-update) | async-done | bytes 338448 | tf_op jit(solution)/shard_map/psum | solution.py:340
  657.3 6.1 scatter_fusion.1
  665.8 241.3 %all-reduce.4.cloned.1.call-done = f32[35712]{0:T(1024)} async-done(((f32[35712]{0:T(1024)}), f32[35712]{0:T(1024)}) %all-reduce.4.cloned.1.call-update) | async-done | bytes 142864 | tf_op jit(solution)/shard_map/psum | solution.py:383
  (715 shorter events, 344.0 us)
Async XLA Ops:
  7.2 62.9 %copy-start = (bf16[128,128]{1,0:T(8,128)(2,1)S(1)}, bf16[128,128]{1,0:T(8,128)(2,1)}, u32[]{:S(2)}) copy-start(bf16[128,128]{1,0:T(8,128)(2,1)} %param.43) | copy-start | bytes 98308
  7.2 638.1 %all-reduce.6.cloned.1.call-start = ((), (), s32[]{:S(2)}) async-start(), calls=%async_computation.1 | async-start | bytes 679936 | tf_op jit(solution)/shard_map/psum | solution.py:340
  8.9 10.7 %copy-start.7 = (f32[512,128]{1,0:T(8,128)}, f32[512,128]{1,0:T(8,128)S(1)}, u32[]{:S(2)}) copy-start(f32[512,128]{1,0:T(8,128)S(1)} %fusion.94) | copy-start | bytes 786436
  9.0 10.7 %copy-start.53 = (s32[1,1,1,512]{3,2,1,0:T(1,128)S(1)}, s32[1,1,1,512]{3,2,1,0:T(1,128)}, u32[]{:S(2)}) copy-start(s32[1,1,1,512]{3,2,1,0:T(1,128)} %param.30) | copy-start | bytes 6148
  10.2 10.6 %copy-start.31 = (s32[1,1,1,512,32]{3,4,2,1,0:T(8,128)S(1)}, s32[1,1,1,512,32]{3,4,2,1,0:T(8,128)}, u32[]{:S(2)}) copy-start(s32[1,1,1,512,32]{3,4,2,1,0:T(8,128)} %param.29) | copy-start | bytes 196612
  10.2 10.7 %copy-start.25 = (s32[1,1,1,1024,32]{3,4,2,1,0:T(8,128)S(1)}, s32[1,1,1,1024,32]{3,4,2,1,0:T(8,128)}, u32[]{:S(2)}) copy-start(s32[1,1,1,1024,32]{3,4,2,1,0:T(8,128)} %param.33) | copy-start | bytes 393220
  13.4 12.0 %copy-start.41 = (s32[1,1,1,8,128]{4,3,2,1,0:T(8,128)S(1)}, s32[1,1,1,8,128]{4,3,2,1,0:T(8,128)}, u32[]{:S(2)}) copy-start(s32[1,1,1,8,128]{4,3,2,1,0:T(8,128)} %param.32) | copy-start | bytes 12292
  13.4 10.2 %collective-permute-start = (bf16[1,3,128,128]{3,2,1,0:T(8,128)(2,1)S(1)}, bf16[1,3,128,128]{3,2,1,0:T(8,128)(2,1)S(1)}, u32[]{:S(2)}, u32[]{:S(2)}) collective-permute-start(bf16[1,3,128,128]{3,2,1,0:T(8,128)(2,1)S(1)} %bitcast.225), channel_id=1, source_target_pairs={{0,8},{8,16},{16,24},{24,32},{32,40},{40,48},{48,56},{56,0},{1,9},... | collective-permute-start | bytes 294920 | tf_op jit(solution)/shard_map/ppermute | solution.py:17
  15.4 8.2 collective-permute-start.1
  19.6 57.3 %copy-start.50 = (bf16[9]{0:T(256)(128)(2,1)}, bf16[9]{0:T(256)(128)(2,1)S(1)}, u32[]{:S(2)}) copy-start(bf16[9]{0:T(256)(128)(2,1)S(1)} %pad.76.clone) | copy-start | bytes 58
  23.7 4.8 collective-permute-start.2
  23.7 4.7 collective-permute-start.3
  28.7 40.2 %copy-start.28 = (bf16[128,128]{1,0:T(8,128)(2,1)S(1)}, bf16[128,128]{1,0:T(8,128)(2,1)}, u32[]{:S(2)}) copy-start(bf16[128,128]{1,0:T(8,128)(2,1)} %param.41) | copy-start | bytes 98308
  28.7 40.4 %copy-start.9 = (bf16[1,1,1,512,128]{4,3,2,1,0:T(8,128)(2,1)S(1)}, bf16[1,1,1,512,128]{4,3,2,1,0:T(8,128)(2,1)}, u32[]{:S(2)}) copy-start(bf16[1,1,1,512,128]{4,3,2,1,0:T(8,128)(2,1)} %param.27) | copy-start | bytes 393220
  28.8 40.4 %copy-start.55 = (bf16[128,128]{1,0:T(8,128)(2,1)S(1)}, bf16[128,128]{1,0:T(8,128)(2,1)}, u32[]{:S(2)}) copy-start(bf16[128,128]{1,0:T(8,128)(2,1)} %param.42) | copy-start | bytes 98308
  70.3 11.7 %copy-start.52 = (f32[1,1,1,1024]{3,2,1,0:T(1,128)S(1)}, f32[1,1,1,1024]{3,2,1,0:T(1,128)}, u32[]{:S(2)}) copy-start(f32[1,1,1,1024]{3,2,1,0:T(1,128)} %param.36) | copy-start | bytes 12292
  73.6 6.6 collective-permute-start.4
  73.7 6.5 collective-permute-start.5
  80.2 4.8 collective-permute-start.6
  80.4 4.6 collective-permute-start.7
  375.0 10.0 %copy-start.35 = (f32[128,128]{1,0:T(8,128)S(1)}, f32[128,128]{1,0:T(8,128)}, u32[]{:S(2)}) copy-start(f32[128,128]{1,0:T(8,128)} %get-tuple-element.466) | copy-start | bytes 196612
  375.0 10.0 %copy-start.36 = (f32[128,128]{1,0:T(8,128)S(1)}, f32[128,128]{1,0:T(8,128)}, u32[]{:S(2)}) copy-start(f32[128,128]{1,0:T(8,128)} %get-tuple-element.467) | copy-start | bytes 196612
  376.3 6.7 collective-permute-start.8
  377.7 5.5 collective-permute-start.9
  383.2 4.8 collective-permute-start.10
  383.4 4.6 collective-permute-start.11
  398.0 509.2 %all-reduce.4.cloned.1.call-start = ((), (), s32[]{:S(2)}) async-start(), calls=%async_computation | async-start | bytes 286720 | tf_op jit(solution)/shard_map/psum | solution.py:383
  645.4 6.7 collective-permute-start.12
  646.9 5.2 collective-permute-start.13
  652.2 4.8 collective-permute-start.14
  652.2 4.7 collective-permute-start.15
  663.5 247.2 %copy-start.21 = (f32[49152]{0:T(1024)S(1)}, f32[49152]{0:T(1024)}, u32[]{:S(2)}) copy-start(f32[49152]{0:T(1024)} %get-tuple-element.474) | copy-start | bytes 589828
  (160 other events, 421.9 us)
Sparse Core Ops, SparseCore 0:
  398.1 247.1 all-reduce.5
  665.2 241.9 all-reduce.3

commit v2 on v1

--- a/solution.py
+++ b/solution.py
@@ -20,6 +20,17 @@
         high = lax.ppermute(lax.slice_in_dim(block, 0, width, axis=dim), axis, backward)
         block = jnp.concatenate([low, block, high], axis=dim)
     return block
+
+
+def summed_everywhere(values, axes):
+    for axis in axes:
+        count = lax.axis_size(axis)
+        stride = 1
+        while stride < count:
+            pairs = [(index, index ^ stride) for index in range(count)]
+            values = values + lax.ppermute(values, axis, pairs)
+            stride *= 2
+    return values
 
 
 def shifted_plus(values):
@@ -337,16 +348,13 @@
     grad_ptable, grad_pradial, grad_pfilter, grad_read, grad_final = lax.scan(
         probe_turn, initial, pieces
     )[0]
-    probe_sums = lax.psum(
-        jnp.concatenate(
-            [
-                grad_pfilter.reshape(-1),
-                grad_read.reshape(-1),
-                grad_pradial.reshape(-1),
-                grad_final.reshape(-1),
-            ]
-        ),
-        ("rep", "gx", "gy"),
+    probe_part = jnp.concatenate(
+        [
+            grad_pfilter.reshape(-1),
+            grad_read.reshape(-1),
+            grad_pradial.reshape(-1),
+            grad_final.reshape(-1),
+        ]
     )
     returned_probe = ghost_grads(
         grad_ptable[atom_count:].reshape(send_rows.shape + (feature_width,))
@@ -358,12 +366,8 @@
     tail_part = jnp.concatenate(
         [grad_mix_first.reshape(-1), grad_mix_second.reshape(-1), grad_proj_probe.reshape(-1)]
     )
-    tail_sums = lax.psum(tail_part, ("rep", "gx", "gy"))
     grad_atable, grad_aradial, grad_afilter = atom_backward(
         tile_nbr, tile_dist, tile_counts, row_table, atom_radial, atom_filter, grad_message
-    )
-    grad_atable, probe_sums, tail_sums = lax.optimization_barrier(
-        (grad_atable, probe_sums, tail_sums)
     )
     returned_atom = ghost_grads(
         grad_atable[atom_count:].reshape(send_rows.shape + (feature_width,))
@@ -380,7 +384,12 @@
             grad_gain.reshape(-1),
         ]
     )
-    atom_sums = lax.psum(atom_part, ("rep", "gx", "gy"))
+    sums = summed_everywhere(
+        jnp.concatenate([probe_part, tail_part, atom_part]), ("gy", "gx", "rep")
+    )
+    probe_sums = sums[: probe_part.shape[0]]
+    tail_sums = sums[probe_part.shape[0] : probe_part.shape[0] + tail_part.shape[0]]
+    atom_sums = sums[probe_part.shape[0] + tail_part.shape[0] :]
     square = feature_width * feature_width
     radial = probe_radial.shape[0] * feature_width
     grad_square = jnp.concatenate(

time: 928 us -> 661 us (0.71)
  waiting for transfers between devices: 385 us -> 123 us
  starting transfers between devices: 23.6 us -> 38.1 us
  between operations: 16 us -> 2.64 us
  loops' own time: 14 us -> 2.67 us
    psum x2 -> x0, waiting for transfers between devices: 366 us -> none  [the longest x1 241 us: per_device(): atom_sums = lax.psum(atom_part, ('rep', 'gx', 'gy'))]
    ppermute x0 -> x8, waiting for transfers between devices: none -> 105 us  [summed_everywhere(): values = values + lax.ppermute(values, axis, pairs)]
    ppermute x0 -> x8, starting transfers between devices: none -> 14.8 us  [summed_everywhere(): values = values + lax.ppermute(values, axis, pairs)]
    another operation x1, loops' own time: 13.6 us -> 2.24 us  [per_device(): lax.scan(probe_turn, initial, pieces)[0]]
  transfers between devices with their start and end apart: 18 -> 24, of which waited for: 10 -> 16; matrix products, arithmetic and copies ran while one was open for 14% -> 2% of each run, Pallas kernels for 0% -> 0%
where the time goes in v2:
time: 661 us; the launch traced here: 648 us
  matrix products  353 us (53%)
  waiting for transfers between devices  123 us (19%)
  local copies, waits for them, and re-layouts  78.6 us (12%)
  other arithmetic  51.3 us (8%)
  starting transfers between devices  38.1 us (6%)
    dot_general x48, matrix products, contract_rows(): lax.dot_general(former, latter, (((0,), (0,)), ((), ())), preferred_eleme...  152 us
    ppermute x8, waiting for transfers between devices, summed_everywhere(): values = values + lax.ppermute(values, axis, pairs)  105 us
    dot_general x16, matrix products, edge_setup(): gathered = jnp.dot(selector, row_table, preferred_element_type=jnp.float32)  98.9 us
    dot_general x16, matrix products, edge_setup(): jnp.dot(hidden, filter_weight, preferred_element_type=jnp.float32)  51.6 us
    dot_general x12, matrix products, edge_backward(): jnp.dot(expansion, grad_pre, preferred_element_type=jnp.float32)  26 us
    convert_element_type x8, other arithmetic, scatter_rows(): high = values.astype(jnp.bfloat16)  22 us
    while x264, local copies, waits for them, and re-layouts  21.2 us
    ppermute x8, starting transfers between devices, with_halo(): lax.ppermute(lax.slice_in_dim(block, 0, width, axis=dim), axis, backward)  16.7 us
  transfers between devices with their start and end apart: 24, of which 16 were waited for; matrix products, arithmetic and copies ran while one was open for 2% of the time, Pallas kernels for 0%

profile of v2, /device:TPU:20, one launch (start us, length us, event | category | flops | bytes accessed | tf_op | source)
XLA Modules:
  0.0 648.5 jit_solution(9828207632790109184)
XLA Ops:
  22.2 40.1 %while.51 = (s32[]{:T(128)}, bf16[4,128,128]{2,1,0:T(8,128)(2,1)S(1)}, s32[4,128,32]{2,1,0:T(8,128)S(1)}, bf16[1536,128]{1,0:T(8,128)(2,1)S(1)}, f32[4,128,32]{2...) while((s32[]{:T(128)}, ...), condition=%wide.region_2.3_spmd, body=%wide.region_0.2_spmd.sunk | while | flops 1778270208 | bytes 5018889 | solution.py:122
  79.4 278.0 %while.52 = (s32[]{:T(128)}, f32[1536,128]{1,0:T(8,128)}, f32[20,128]{1,0:T(8,128)}, f32[128,128]{1,0:T(8,128)}, f32[128,128]{1,0:T(8,128)}, /*index=5*/f32[128]...) while((s32[]{:T(128)}, f32[1536,128]{1,0:T(8,128)}, ...), condition=%wide.region_6.7_spmd.clone, body=%wide.region_3.6_spmd.clone.sunk | while | flops 5324391424 | bytes 60448700 | solution.py:348
  85.2 6.5 fusion.232
  99.6 7.5 %fusion.236 = f32[1536,256]{1,0:T(8,128)S(1)} fusion(s32[4096]{0:T(1024)S(1)} %eq.208, bf16[4096,128]{1,0:T(8,128)(2,1)S(1)} %get-tuple-element.888, bf16[4096,128]{1,0:T(8,128)(2,1)S(1)} %get-tuple-element.889), kind=kOutput, calls=%fused_computation.31.clone.1 | convolution fusion | flops 3231711232 | bytes 3686400 | tf_op jit(solution)/shard_map/while/body/eval_jaxpr/dot_general | solution.py:41
  119.9 6.5 fusion.232
  134.3 7.5 %fusion.236 = f32[1536,256]{1,0:T(8,128)S(1)} fusion(s32[4096]{0:T(1024)S(1)} %eq.208, bf16[4096,128]{1,0:T(8,128)(2,1)S(1)} %get-tuple-element.888, bf16[4096,128]{1,0:T(8,128)(2,1)S(1)} %get-tuple-element.889), kind=kOutput, calls=%fused_computation.31.clone.1 | convolution fusion | flops 3231711232 | bytes 3686400 | tf_op jit(solution)/shard_map/while/body/eval_jaxpr/dot_general | solution.py:41
  154.6 6.5 fusion.232
  168.9 7.5 %fusion.236 = f32[1536,256]{1,0:T(8,128)S(1)} fusion(s32[4096]{0:T(1024)S(1)} %eq.208, bf16[4096,128]{1,0:T(8,128)(2,1)S(1)} %get-tuple-element.888, bf16[4096,128]{1,0:T(8,128)(2,1)S(1)} %get-tuple-element.889), kind=kOutput, calls=%fused_computation.31.clone.1 | convolution fusion | flops 3231711232 | bytes 3686400 | tf_op jit(solution)/shard_map/while/body/eval_jaxpr/dot_general | solution.py:41
  189.2 6.5 fusion.232
  203.6 7.5 %fusion.236 = f32[1536,256]{1,0:T(8,128)S(1)} fusion(s32[4096]{0:T(1024)S(1)} %eq.208, bf16[4096,128]{1,0:T(8,128)(2,1)S(1)} %get-tuple-element.888, bf16[4096,128]{1,0:T(8,128)(2,1)S(1)} %get-tuple-element.889), kind=kOutput, calls=%fused_computation.31.clone.1 | convolution fusion | flops 3231711232 | bytes 3686400 | tf_op jit(solution)/shard_map/while/body/eval_jaxpr/dot_general | solution.py:41
  223.9 6.5 fusion.232
  238.3 7.5 %fusion.236 = f32[1536,256]{1,0:T(8,128)S(1)} fusion(s32[4096]{0:T(1024)S(1)} %eq.208, bf16[4096,128]{1,0:T(8,128)(2,1)S(1)} %get-tuple-element.888, bf16[4096,128]{1,0:T(8,128)(2,1)S(1)} %get-tuple-element.889), kind=kOutput, calls=%fused_computation.31.clone.1 | convolution fusion | flops 3231711232 | bytes 3686400 | tf_op jit(solution)/shard_map/while/body/eval_jaxpr/dot_general | solution.py:41
  258.6 6.5 fusion.232
  273.0 7.5 %fusion.236 = f32[1536,256]{1,0:T(8,128)S(1)} fusion(s32[4096]{0:T(1024)S(1)} %eq.208, bf16[4096,128]{1,0:T(8,128)(2,1)S(1)} %get-tuple-element.888, bf16[4096,128]{1,0:T(8,128)(2,1)S(1)} %get-tuple-element.889), kind=kOutput, calls=%fused_computation.31.clone.1 | convolution fusion | flops 3231711232 | bytes 3686400 | tf_op jit(solution)/shard_map/while/body/eval_jaxpr/dot_general | solution.py:41
  293.3 6.5 fusion.232
  307.7 7.5 %fusion.236 = f32[1536,256]{1,0:T(8,128)S(1)} fusion(s32[4096]{0:T(1024)S(1)} %eq.208, bf16[4096,128]{1,0:T(8,128)(2,1)S(1)} %get-tuple-element.888, bf16[4096,128]{1,0:T(8,128)(2,1)S(1)} %get-tuple-element.889), kind=kOutput, calls=%fused_computation.31.clone.1 | convolution fusion | flops 3231711232 | bytes 3686400 | tf_op jit(solution)/shard_map/while/body/eval_jaxpr/dot_general | solution.py:41
  328.0 6.5 fusion.232
  342.3 7.5 %fusion.236 = f32[1536,256]{1,0:T(8,128)S(1)} fusion(s32[4096]{0:T(1024)S(1)} %eq.208, bf16[4096,128]{1,0:T(8,128)(2,1)S(1)} %get-tuple-element.888, bf16[4096,128]{1,0:T(8,128)(2,1)S(1)} %get-tuple-element.889), kind=kOutput, calls=%fused_computation.31.clone.1 | convolution fusion | flops 3231711232 | bytes 3686400 | tf_op jit(solution)/shard_map/while/body/eval_jaxpr/dot_general | solution.py:41
  372.5 6.1 scatter_fusion
  382.8 122.3 %while.53 = (s32[]{:T(128)}, f32[1536,128]{1,0:T(8,128)S(1)}, f32[20,128]{1,0:T(8,128)S(1)}, f32[128,128]{1,0:T(8,128)}, s32[4,128,32]{2,1,0:T(8,128)S(1)}, /*in...) while((s32[]{:T(128)}, f32[1536,128]{1,0:T(8,128)S(1)}, ...), condition=%wide.region_9.10_spmd.clone, body=%wide.region_8.9_spmd.clone.sunk | while | flops 5316695040 | bytes 50439636 | solution.py:148
  401.4 6.5 fusion.254
  432.0 6.5 fusion.254
  462.6 6.5 fusion.254
  493.1 6.5 fusion.254
  518.4 6.1 scatter_fusion.1
  532.0 11.6 %collective-permute-done.17 = f32[120320]{0:T(1024)S(1)} collective-permute-done((f32[120320]{0:T(1024)S(1)}, f32[120320]{0:T(1024)S(1)}, u32[]{:S(2)}, u32[]{:S(2)}) %collective-permute-start.17) | collective-permute-done | bytes 481312 | tf_op jit(solution)/shard_map/ppermute | solution.py:31
  544.4 13.7 %collective-permute-done.18 = f32[120320]{0:T(1024)S(1)} collective-permute-done((f32[120320]{0:T(1024)S(1)}, f32[120320]{0:T(1024)S(1)}, u32[]{:S(2)}, u32[]{:S(2)}) %collective-permute-start.18) | collective-permute-done | bytes 481312 | tf_op jit(solution)/shard_map/ppermute | solution.py:31
  560.1 10.1 %collective-permute-done.19 = f32[120320]{0:T(1024)S(1)} collective-permute-done((f32[120320]{0:T(1024)S(1)}, f32[120320]{0:T(1024)S(1)}, u32[]{:S(2)}, u32[]{:S(2)}) %collective-permute-start.19) | collective-permute-done | bytes 481312 | tf_op jit(solution)/shard_map/ppermute | solution.py:31
  573.1 19.8 %collective-permute-done.20 = f32[120320]{0:T(1024)S(1)} collective-permute-done((f32[120320]{0:T(1024)S(1)}, f32[120320]{0:T(1024)S(1)}, u32[]{:S(2)}, u32[]{:S(2)}) %collective-permute-start.20) | collective-permute-done | bytes 481312 | tf_op jit(solution)/shard_map/ppermute | solution.py:31
  595.4 23.8 %collective-permute-done.21 = f32[120320]{0:T(1024)S(1)} collective-permute-done((f32[120320]{0:T(1024)S(1)}, f32[120320]{0:T(1024)S(1)}, u32[]{:S(2)}, u32[]{:S(2)}) %collective-permute-start.21) | collective-permute-done | bytes 481312 | tf_op jit(solution)/shard_map/ppermute | solution.py:31
  620.5 11.8 %collective-permute-done.22 = f32[120320]{0:T(1024)S(1)} collective-permute-done((f32[120320]{0:T(1024)S(1)}, f32[120320]{0:T(1024)S(1)}, u32[]{:S(2)}, u32[]{:S(2)}) %collective-permute-start.22) | collective-permute-done | bytes 481312 | tf_op jit(solution)/shard_map/ppermute | solution.py:31
  633.7 12.4 %collective-permute-done.23 = f32[120320]{0:T(1024)S(1)} collective-permute-done((f32[120320]{0:T(1024)S(1)}, f32[120320]{0:T(1024)S(1)}, u32[]{:S(2)}, u32[]{:S(2)}) %collective-permute-start.23) | collective-permute-done | bytes 481312 | tf_op jit(solution)/shard_map/ppermute | solution.py:31
  (744 shorter events, 390.4 us)
Async XLA Ops:
  0.6 62.9 %copy-start = (bf16[128,128]{1,0:T(8,128)(2,1)S(1)}, bf16[128,128]{1,0:T(8,128)(2,1)}, u32[]{:S(2)}) copy-start(bf16[128,128]{1,0:T(8,128)(2,1)} %param.43) | copy-start | bytes 98308
  6.9 12.0 %copy-start.40 = (s32[1,1,1,8,128]{4,3,2,1,0:T(8,128)S(1)}, s32[1,1,1,8,128]{4,3,2,1,0:T(8,128)}, u32[]{:S(2)}) copy-start(s32[1,1,1,8,128]{4,3,2,1,0:T(8,128)} %param.32) | copy-start | bytes 12292
  6.9 10.2 %collective-permute-start = (bf16[1,3,128,128]{3,2,1,0:T(8,128)(2,1)S(1)}, bf16[1,3,128,128]{3,2,1,0:T(8,128)(2,1)S(1)}, u32[]{:S(2)}, u32[]{:S(2)}) collective-permute-start(bf16[1,3,128,128]{3,2,1,0:T(8,128)(2,1)S(1)} %bitcast.230), channel_id=1, source_target_pairs={{0,8},{8,16},{16,24},{24,32},{32,40},{40,48},{48,56},{56,0},{1,9},... | collective-permute-start | bytes 294920 | tf_op jit(solution)/shard_map/ppermute | solution.py:17
  8.9 8.2 %collective-permute-start.1 = (bf16[1,3,128,128]{3,2,1,0:T(8,128)(2,1)S(1)}, bf16[1,3,128,128]{3,2,1,0:T(8,128)(2,1)S(1)}, u32[]{:S(2)}, u32[]{:S(2)}) collective-permute-start(bf16[1,3,128,128]{3,2,1,0:T(8,128)(2,1)S(1)} %bitcast.229), channel_id=1, source_target_pairs={{8,0},{16,8},{24,16},{32,24},{40,32},{48,40},{56,48},{0,56},{9,1},... | collective-permute-start | bytes 294920 | tf_op jit(solution)/shard_map/ppermute | solution.py:20
  13.0 57.3 %copy-start.52 = (bf16[9]{0:T(256)(128)(2,1)}, bf16[9]{0:T(256)(128)(2,1)S(1)}, u32[]{:S(2)}) copy-start(bf16[9]{0:T(256)(128)(2,1)S(1)} %pad.65.clone) | copy-start | bytes 58
  17.1 4.8 collective-permute-start.2
  17.2 4.7 collective-permute-start.3
  22.2 40.2 %copy-start.29 = (bf16[128,128]{1,0:T(8,128)(2,1)S(1)}, bf16[128,128]{1,0:T(8,128)(2,1)}, u32[]{:S(2)}) copy-start(bf16[128,128]{1,0:T(8,128)(2,1)} %param.41) | copy-start | bytes 98308
  22.2 40.3 %copy-start.9 = (bf16[1,1,1,512,128]{4,3,2,1,0:T(8,128)(2,1)S(1)}, bf16[1,1,1,512,128]{4,3,2,1,0:T(8,128)(2,1)}, u32[]{:S(2)}) copy-start(bf16[1,1,1,512,128]{4,3,2,1,0:T(8,128)(2,1)} %param.27) | copy-start | bytes 393220
  22.2 40.3 %copy-start.57 = (bf16[128,128]{1,0:T(8,128)(2,1)S(1)}, bf16[128,128]{1,0:T(8,128)(2,1)}, u32[]{:S(2)}) copy-start(bf16[128,128]{1,0:T(8,128)(2,1)} %param.42) | copy-start | bytes 98308
  67.0 6.6 %collective-permute-start.4 = (bf16[1,3,128,128]{3,2,1,0:T(8,128)(2,1)S(1)}, bf16[1,3,128,128]{3,2,1,0:T(8,128)(2,1)S(1)}, u32[]{:S(2)}, u32[]{:S(2)}) collective-permute-start(bf16[1,3,128,128]{3,2,1,0:T(8,128)(2,1)S(1)} %bitcast.236), channel_id=1, source_target_pairs={{0,8},{8,16},{16,24},{24,32},{32,40},{40,48},{48,56},{56,0},{1,9},... | collective-permute-start | bytes 294920 | tf_op jit(solution)/shard_map/ppermute | solution.py:17
  67.1 6.5 %collective-permute-start.5 = (bf16[1,3,128,128]{3,2,1,0:T(8,128)(2,1)S(1)}, bf16[1,3,128,128]{3,2,1,0:T(8,128)(2,1)S(1)}, u32[]{:S(2)}, u32[]{:S(2)}) collective-permute-start(bf16[1,3,128,128]{3,2,1,0:T(8,128)(2,1)S(1)} %bitcast.235), channel_id=1, source_target_pairs={{8,0},{16,8},{24,16},{32,24},{40,32},{48,40},{56,48},{0,56},{9,1},... | collective-permute-start | bytes 294920 | tf_op jit(solution)/shard_map/ppermute | solution.py:20
  73.6 4.8 collective-permute-start.6
  73.8 4.6 collective-permute-start.7
  357.4 13.0 %copy-start.43 = (f32[128]{0:T(128)S(1)}, f32[128]{0:T(128)}, u32[]{:S(2)}) copy-start(f32[128]{0:T(128)} %get-tuple-element.466) | copy-start | bytes 1540
  359.3 6.6 %collective-permute-start.8 = (bf16[1,3,128,128]{3,2,1,0:T(8,128)(2,1)S(1)}, bf16[1,3,128,128]{3,2,1,0:T(8,128)(2,1)S(1)}, u32[]{:S(2)}, u32[]{:S(2)}) collective-permute-start(bf16[1,3,128,128]{3,2,1,0:T(8,128)(2,1)S(1)} %bitcast.234), channel_id=1, source_target_pairs={{0,8},{8,16},{16,24},{24,32},{32,40},{40,48},{48,56},{56,0},{1,9},... | collective-permute-start | bytes 294920 | tf_op jit(solution)/shard_map/ppermute | solution.py:17
  360.7 5.6 collective-permute-start.9
  366.3 5.4 collective-permute-start.10
  366.5 5.3 collective-permute-start.11
  505.3 6.0 collective-permute-start.12
  508.1 5.1 collective-permute-start.13
  513.2 4.8 collective-permute-start.14
  513.3 4.7 collective-permute-start.15
  525.5 1.9 collective-permute-start.16
  527.5 16.1 %collective-permute-start.17 = (f32[120320]{0:T(1024)S(1)}, f32[120320]{0:T(1024)S(1)}, u32[]{:S(2)}, u32[]{:S(2)}) collective-permute-start(f32[120320]{0:T(1024)S(1)} %add.253), channel_id=1, source_target_pairs={{0,2},{1,3},{2,0},{3,1},{4,6},{5,7},{6,4},{7,5},{8,10},{9,11},{10,... | collective-permute-start | bytes 1443848 | tf_op jit(solution)/shard_map/ppermute | solution.py:31
  543.7 14.3 %collective-permute-start.18 = (f32[120320]{0:T(1024)S(1)}, f32[120320]{0:T(1024)S(1)}, u32[]{:S(2)}, u32[]{:S(2)}) collective-permute-start(f32[120320]{0:T(1024)S(1)} %add.254), channel_id=1, source_target_pairs={{0,4},{1,5},{2,6},{3,7},{4,0},{5,1},{6,2},{7,3},{8,12},{9,13},{10,... | collective-permute-start | bytes 1443848 | tf_op jit(solution)/shard_map/ppermute | solution.py:31
  558.1 12.2 %collective-permute-start.19 = (f32[120320]{0:T(1024)S(1)}, f32[120320]{0:T(1024)S(1)}, u32[]{:S(2)}, u32[]{:S(2)}) collective-permute-start(f32[120320]{0:T(1024)S(1)} %add.255), channel_id=1, source_target_pairs={{0,8},{8,0},{16,24},{24,16},{32,40},{40,32},{48,56},{56,48},{1,9},... | collective-permute-start | bytes 1443848 | tf_op jit(solution)/shard_map/ppermute | solution.py:31
  570.3 62.7 %copy-start.12 = (f32[512,128]{1,0:T(8,128)S(1)}, f32[512,128]{1,0:T(8,128)}, u32[]{:S(2)}) copy-start(f32[512,128]{1,0:T(8,128)} %copy-done.11) | copy-start | bytes 786436
  570.3 22.5 %collective-permute-start.20 = (f32[120320]{0:T(1024)S(1)}, f32[120320]{0:T(1024)S(1)}, u32[]{:S(2)}, u32[]{:S(2)}) collective-permute-start(f32[120320]{0:T(1024)S(1)} %add.256), channel_id=1, source_target_pairs={{0,16},{8,24},{16,0},{24,8},{32,48},{40,56},{48,32},{56,40},{1,17}... | collective-permute-start | bytes 1443848 | tf_op jit(solution)/shard_map/ppermute | solution.py:31
  592.9 26.3 %collective-permute-start.21 = (f32[120320]{0:T(1024)S(1)}, f32[120320]{0:T(1024)S(1)}, u32[]{:S(2)}, u32[]{:S(2)}) collective-permute-start(f32[120320]{0:T(1024)S(1)} %add.257), channel_id=1, source_target_pairs={{0,32},{8,40},{16,48},{24,56},{32,0},{40,8},{48,16},{56,24},{1,33}... | collective-permute-start | bytes 1443848 | tf_op jit(solution)/shard_map/ppermute | solution.py:31
  619.3 13.1 %collective-permute-start.22 = (f32[120320]{0:T(1024)S(1)}, f32[120320]{0:T(1024)S(1)}, u32[]{:S(2)}, u32[]{:S(2)}) collective-permute-start(f32[120320]{0:T(1024)S(1)} %add.258), channel_id=1, source_target_pairs={{0,64},{64,0},{128,192},{192,128},{1,65},{65,1},{129,193},{193,129... | collective-permute-start | bytes 1443848 | tf_op jit(solution)/shard_map/ppermute | solution.py:31
  632.4 13.7 %collective-permute-start.23 = (f32[120320]{0:T(1024)S(1)}, f32[120320]{0:T(1024)S(1)}, u32[]{:S(2)}, u32[]{:S(2)}) collective-permute-start(f32[120320]{0:T(1024)S(1)} %add.259), channel_id=1, source_target_pairs={{0,128},{64,192},{128,0},{192,64},{1,129},{65,193},{129,1},{193,65... | collective-permute-start | bytes 1443848 | tf_op jit(solution)/shard_map/ppermute | solution.py:31
  (168 other events, 495.0 us)
